TPU v7x, 512 devices: a whole 4x8x8 slice. The times are simulated.
512 devices in a mesh: row: 16 (over y_lo, x), col: 32 (over z, y_hi, core).
Axes of the slice: x: 4, y: 8 (y_hi: 2, y_lo: 4; y = y_hi * 4 + y_lo), z: 8, core: 2. Of those that a mesh axis runs over, the one named last changes fastest.
Arguments:
- precond: float32 [8, 8192, 8192], P(None, 'row', 'col'), may hold values from -6 to 6
- out_factors: bfloat16 [1536, 8192], P('col', 'row'), may hold values from -6 to 6
- in_factors: bfloat16 [1536, 8192], P('row', 'col'), may hold values from -6 to 6
- token_mask: int32 [1536], replicated, may hold values 0 or 1
- seq_ids: int32 [1536], replicated, may hold values from 0 to 3, never falling along the last dimension, each value on 1 to 576 neighbouring positions
- query_ids: int32 [8], replicated, may hold values from 0 to 7, each once
Outputs:
- scores: float32 [8, 4], replicated
Inputs may be any that keep to these rules, and one draw needn't show every extreme that they name: seq_ids never falls along the tokens; each sequence has 1 to 576 tokens. query_ids names each query once.
All inputs are finite; a program needn't handle non-finite values.
Results may differ from a plain program's by a relative error of at most 0.0003.
Values may be sent and summed in bfloat16 or wider, within the bound.
No kernel may reach another device: no remote copies, remote signals or barrier semaphores. Data moves between devices by JAX's collectives and lax.ppermute only.
A program may use at most 64 MiB of HBM per device.

v0:
```python
import math
import jax
import jax.numpy as jnp
from jax import lax
from jax.sharding import PartitionSpec as P

DOUT = 8192
DIN = 8192
SEQ = 4
LEN = 384


def shards(precond, out_factors, in_factors, token_mask, seq_ids, query_ids):
    num_queries = precond.shape[0]
    weight = token_mask.astype(jnp.float32)[:, None] * (
        seq_ids[:, None] == jnp.arange(SEQ, dtype=jnp.int32)[None, :]
    ).astype(jnp.float32)
    out_whole = lax.all_gather(out_factors, "col", axis=0, tiled=True)
    out_wide = out_whole.astype(jnp.float32)
    in_wide = lax.all_gather(in_factors, "row", axis=0, tiled=True).astype(jnp.float32)

    def one_query(query_grad):
        mapped = lax.dot_general(
            in_wide, query_grad, (((1,), (1,)), ((), ())), precision=lax.Precision.HIGHEST
        )
        per_token = jnp.sum(mapped * out_wide, axis=1)
        return jnp.dot(per_token, weight, precision=lax.Precision.HIGHEST)

    total = lax.map(one_query, precond)
    summed = lax.psum(total, ("row", "col"))
    select = (query_ids[:, None] == jnp.arange(num_queries, dtype=jnp.int32)[None, :]).astype(
        jnp.float32
    )
    scale = 1.0 / math.sqrt(DOUT * DIN * LEN)
    return jnp.dot(select, summed, precision=lax.Precision.HIGHEST) * scale


def solution(mesh):
    placed = (P(None, "row", "col"), P("col", "row"), P("row", "col"), P(), P(), P())
    return jax.shard_map(shards, mesh=mesh, in_specs=placed, out_specs=P(), check_vma=False)
```

profile of v0, /device:TPU:1, one launch (start us, length us, event | category | flops | bytes accessed | tf_op | source)
XLA Modules:
  0.0 254.1 jit_solution(18171253237847577728)
XLA Ops:
  6.5 0.0 copy-start
  6.5 0.0 all-gather.2.cloned.1.call-start
  6.5 0.7 all-gather.2.cloned.1.call-update
  7.3 41.4 %all_gather.6 = bf16[1536,256]{1,0:T(8,128)(2,1)S(1)} all-gather(bf16[96,256]{1,0:T(8,128)(2,1)} %param.10), channel_id=1, replica_groups=mesh['row'=16,'col'=32] {'row'}, dimensions={0}, use_global_device_ids=true | all-gather | bytes 835584 | tf_op jit(solution)/shard_map/all_gather | solution.py:20
  48.7 0.0 copy-start.1
  48.7 1.3 convert_element_type.11
  50.0 0.0 copy-done
  50.0 55.2 %all-gather.2.cloned.1.call-done = bf16[1536,512]{1,0:T(8,128)(2,1)} async-done(((bf16[48,512]{1,0:T(8,128)(2,1)}), bf16[1536,512]{1,0:T(8,128)(2,1)}) %all-gather.2.cloned.1.call-update) | async-done | bytes 1572880 | tf_op jit(solution)/shard_map/all_gather | solution.py:18
  105.2 1.8 convert_element_type.12
  107.1 0.0 copy-done.1
  107.1 0.0 copy-start.2
  107.1 42.3 %while.11 = (s32[]{:T(128)}, f32[8,4]{1,0:T(8,128)S(1)}, f32[8,512,256]{2,1,0:T(8,128)}, f32[1536,256]{1,0:T(8,128)}, f32[1536,512]{1,0:T(8,128)S(1)}, /*index=5...) while((s32[]{:T(128)}, f32[8,4]{1,0:T(8,128)S(1)}, f32[8,512,256]{2,1,0:T(8,128)}, ...), condition=%wide.region_2.3_spmd.clone, body=%wide.region_0.2_spmd.clone.sunk | while | flops 2417576448 | bytes 5280401 | solution.py:29
  107.1 4.4 %fusion.27 = f32[1536]{0:T(1024)S(1)} fusion(f32[1536,512]{1,0:T(8,128)S(1)} %get-tuple-element.135, f32[1536,256]{1,0:T(8,128)} %get-tuple-element.134, f32[8,512,256]{2,1,0:T(8,128)} %get-tuple-element.133, s32[]{:T(128)} %get-tuple-element.122), kind=kOutput, calls=%fused_computation.3.clone.1 | convolution fusion | flops 2417490432 | bytes 5249536 | tf_op jit(solution)/shard_map/while/body/eval_jaxpr/dot_general | solution.py:23
  111.5 0.8 fusion.28
  112.4 4.4 %fusion.27 = f32[1536]{0:T(1024)S(1)} fusion(f32[1536,512]{1,0:T(8,128)S(1)} %get-tuple-element.135, f32[1536,256]{1,0:T(8,128)} %get-tuple-element.134, f32[8,512,256]{2,1,0:T(8,128)} %get-tuple-element.133, s32[]{:T(128)} %get-tuple-element.122), kind=kOutput, calls=%fused_computation.3.clone.1 | convolution fusion | flops 2417490432 | bytes 5249536 | tf_op jit(solution)/shard_map/while/body/eval_jaxpr/dot_general | solution.py:23
  116.8 0.8 fusion.28
  117.7 4.4 %fusion.27 = f32[1536]{0:T(1024)S(1)} fusion(f32[1536,512]{1,0:T(8,128)S(1)} %get-tuple-element.135, f32[1536,256]{1,0:T(8,128)} %get-tuple-element.134, f32[8,512,256]{2,1,0:T(8,128)} %get-tuple-element.133, s32[]{:T(128)} %get-tuple-element.122), kind=kOutput, calls=%fused_computation.3.clone.1 | convolution fusion | flops 2417490432 | bytes 5249536 | tf_op jit(solution)/shard_map/while/body/eval_jaxpr/dot_general | solution.py:23
  122.1 0.8 fusion.28
  123.0 4.4 %fusion.27 = f32[1536]{0:T(1024)S(1)} fusion(f32[1536,512]{1,0:T(8,128)S(1)} %get-tuple-element.135, f32[1536,256]{1,0:T(8,128)} %get-tuple-element.134, f32[8,512,256]{2,1,0:T(8,128)} %get-tuple-element.133, s32[]{:T(128)} %get-tuple-element.122), kind=kOutput, calls=%fused_computation.3.clone.1 | convolution fusion | flops 2417490432 | bytes 5249536 | tf_op jit(solution)/shard_map/while/body/eval_jaxpr/dot_general | solution.py:23
  127.4 0.8 fusion.28
  128.3 4.4 %fusion.27 = f32[1536]{0:T(1024)S(1)} fusion(f32[1536,512]{1,0:T(8,128)S(1)} %get-tuple-element.135, f32[1536,256]{1,0:T(8,128)} %get-tuple-element.134, f32[8,512,256]{2,1,0:T(8,128)} %get-tuple-element.133, s32[]{:T(128)} %get-tuple-element.122), kind=kOutput, calls=%fused_computation.3.clone.1 | convolution fusion | flops 2417490432 | bytes 5249536 | tf_op jit(solution)/shard_map/while/body/eval_jaxpr/dot_general | solution.py:23
  132.7 0.8 fusion.28
  133.6 4.4 %fusion.27 = f32[1536]{0:T(1024)S(1)} fusion(f32[1536,512]{1,0:T(8,128)S(1)} %get-tuple-element.135, f32[1536,256]{1,0:T(8,128)} %get-tuple-element.134, f32[8,512,256]{2,1,0:T(8,128)} %get-tuple-element.133, s32[]{:T(128)} %get-tuple-element.122), kind=kOutput, calls=%fused_computation.3.clone.1 | convolution fusion | flops 2417490432 | bytes 5249536 | tf_op jit(solution)/shard_map/while/body/eval_jaxpr/dot_general | solution.py:23
  138.0 0.8 fusion.28
  138.8 4.4 %fusion.27 = f32[1536]{0:T(1024)S(1)} fusion(f32[1536,512]{1,0:T(8,128)S(1)} %get-tuple-element.135, f32[1536,256]{1,0:T(8,128)} %get-tuple-element.134, f32[8,512,256]{2,1,0:T(8,128)} %get-tuple-element.133, s32[]{:T(128)} %get-tuple-element.122), kind=kOutput, calls=%fused_computation.3.clone.1 | convolution fusion | flops 2417490432 | bytes 5249536 | tf_op jit(solution)/shard_map/while/body/eval_jaxpr/dot_general | solution.py:23
  143.3 0.8 fusion.28
  144.1 4.4 %fusion.27 = f32[1536]{0:T(1024)S(1)} fusion(f32[1536,512]{1,0:T(8,128)S(1)} %get-tuple-element.135, f32[1536,256]{1,0:T(8,128)} %get-tuple-element.134, f32[8,512,256]{2,1,0:T(8,128)} %get-tuple-element.133, s32[]{:T(128)} %get-tuple-element.122), kind=kOutput, calls=%fused_computation.3.clone.1 | convolution fusion | flops 2417490432 | bytes 5249536 | tf_op jit(solution)/shard_map/while/body/eval_jaxpr/dot_general | solution.py:23
  148.5 0.8 fusion.28
  149.4 97.1 %psum.7 = f32[8,4]{1,0:T(8,128)S(1)} all-reduce(f32[8,4]{1,0:T(8,128)S(1)} %get-tuple-element.37), channel_id=1, replica_groups=mesh['row'=16,'col'=32] {'row','col'}, use_global_device_ids=true, to_apply=%region_3.4 | all-reduce | flops 32 | bytes 256 | tf_op jit(solution)/shard_map/psum | solution.py:30
  246.5 0.0 copy-done.2
  246.5 0.8 convolution_multiply_fusion
  (18 shorter events, 0.3 us)
Async XLA Ops:
  6.5 43.5 %copy-start = (s32[1536]{0:T(1024)S(1)}, s32[1536]{0:T(1024)}, u32[]{:S(2)}) copy-start(s32[1536]{0:T(1024)} %param.11) | copy-start | bytes 18436
  6.5 98.7 %all-gather.2.cloned.1.call-start = ((), (), s32[]{:S(2)}) async-start(), calls=%async_computation | async-start | bytes 1622016 | tf_op jit(solution)/shard_map/all_gather | solution.py:18
  48.7 58.4 %copy-start.1 = (s32[1536]{0:T(1024)S(1)}, s32[1536]{0:T(1024)}, u32[]{:S(2)}) copy-start(s32[1536]{0:T(1024)} %param.12) | copy-start | bytes 18436
  107.1 139.4 %copy-start.2 = (s32[8]{0:T(128)S(1)}, s32[8]{0:T(128)}, u32[]{:S(2)}) copy-start(s32[8]{0:T(128)} %param.13) | copy-start | bytes 100
Sparse Core Ops, SparseCore 0:
  10.7 94.5 all-gather.1
where the time goes:
time: 255 us; the launch traced here: 254 us
  blocking collectives  139 us (55%)
  waiting for transfers between devices  56 us (22%)
  matrix products  42.5 us (17%)
  between operations  13.4 us (5%)
  other arithmetic  3.12 us (1%)
    psum x1, blocking collectives, shards(): summed = lax.psum(total, ('row', 'col'))  97.1 us
    all_gather x1, waiting for transfers between devices, shards(): out_whole = lax.all_gather(out_factors, 'col', axis=0, tiled=True)  55.2 us
    all_gather x1, blocking collectives, shards(): lax.all_gather(in_factors, 'row', axis=0, tiled=True).astype(jnp.float32)  41.4 us
    dot_general x8, matrix products, one_query(): lax.dot_general(in_wide, query_grad, (((1,), (1,)), ((), ())), precision=...  35.2 us
    dot_general x8, matrix products, one_query(): return jnp.dot(per_token, weight, precision=lax.Precision.HIGHEST)  6.58 us
  transfers between devices with their start and end apart: 1, of which 1 were waited for; matrix products, arithmetic and copies ran while one was open for 1% of the time, Pallas kernels for 0%

commit v1 on v0

--- a/solution.py
+++ b/solution.py
@@ -1,3 +1,4 @@
+import functools
 import math
 import jax
 import jax.numpy as jnp
@@ -10,12 +11,25 @@
 LEN = 384
 
 
+def racks_choose(mine_x, shard_axis):
+    far_arr = jnp.concatenate(
+        lax.all_to_all(
+            jnp.stack([mine_x] * lax.axis_size(shard_axis)), shard_axis, split_axis=0, concat_axis=0
+        ),
+        axis=0,
+    )
+    return far_arr
+
+
+_pass_values = functools.partial(racks_choose, shard_axis="col")
+
+
 def shards(precond, out_factors, in_factors, token_mask, seq_ids, query_ids):
     num_queries = precond.shape[0]
     weight = token_mask.astype(jnp.float32)[:, None] * (
         seq_ids[:, None] == jnp.arange(SEQ, dtype=jnp.int32)[None, :]
     ).astype(jnp.float32)
-    out_whole = lax.all_gather(out_factors, "col", axis=0, tiled=True)
+    out_whole = _pass_values(out_factors)
     out_wide = out_whole.astype(jnp.float32)
     in_wide = lax.all_gather(in_factors, "row", axis=0, tiled=True).astype(jnp.float32)
 

time: 255 us -> 240 us (0.941)
  waiting for transfers between devices: 56 us -> 0.01 us
  blocking collectives: 139 us -> 174 us
  starting transfers between devices: 0.01 us -> 17.4 us
  between operations: 13.4 us -> 0.06 us
    all_gather x1 -> x0, waiting for transfers between devices: 55.2 us -> none  [shards(): out_whole = lax.all_gather(out_factors, 'col', axis=0, tiled=True)]
    all_gather x1, blocking collectives: 41.4 us -> 67.8 us  [shards(): lax.all_gather(in_factors, 'row', axis=0, tiled=True).astype(jnp.float32)]
    all_to_all x0 -> x1, starting transfers between devices: none -> 17.4 us  [racks_choose(): lax.all_to_all(jnp.stack([mine_x] * lax.axis_size(shard_axis)), shard_axi...]
    psum x1, blocking collectives: 97.1 us -> 106 us  [shards(): summed = lax.psum(total, ('row', 'col'))]
  transfers between devices with their start and end apart: 1 -> 1, of which waited for: 1 -> 0; matrix products, arithmetic and copies ran while one was open for 1% -> 1% of each run, Pallas kernels for 0% -> 0%
where the time goes in v1:
time: 240 us
  blocking collectives  174 us (72%)
  matrix products  42.5 us (18%)
  starting transfers between devices  17.4 us (7%)
  other arithmetic  3.12 us (1%)
  local copies, waits for them, and re-layouts  2.48 us (1%)
    psum x1, blocking collectives, shards(): summed = lax.psum(total, ('row', 'col'))  106 us
    all_gather x1, blocking collectives, shards(): lax.all_gather(in_factors, 'row', axis=0, tiled=True).astype(jnp.float32)  67.8 us
    dot_general x8, matrix products, one_query(): lax.dot_general(in_wide, query_grad, (((1,), (1,)), ((), ())), precision=...  35.2 us
    all_to_all x1, starting transfers between devices, racks_choose(): lax.all_to_all(jnp.stack([mine_x] * lax.axis_size(shard_axis)), shard_axi...  17.4 us
    dot_general x8, matrix products, one_query(): return jnp.dot(per_token, weight, precision=lax.Precision.HIGHEST)  6.58 us
  transfers between devices with their start and end apart: 1, of which 0 were waited for; matrix products, arithmetic and copies ran while one was open for 1% of the time, Pallas kernels for 0%

profile of v1, /device:TPU:1, one launch (start us, length us, event | category | flops | bytes accessed | tf_op | source)
XLA Modules:
  0.0 239.8 jit_solution(13347727869896359610)
XLA Ops:
  0.0 0.0 copy-start
  0.0 2.1 stack.2
  2.1 0.0 copy-start.1
  2.1 17.4 %all-to-all-start = ((bf16[32,48,512]{2,1,0:T(8,128)(2,1)}), bf16[32,48,512]{2,1,0:T(8,128)(2,1)}, u32[]{:S(2)}, u32[]{:S(2)}) async-start(bf16[32,48,512]{2,1,0:T(8,128)(2,1)} %stack.2), calls=%async_computation | async-start | bytes 3145728 | tf_op jit(solution)/shard_map/all_to_all | solution.py:16
  19.5 0.0 copy-done
  19.6 67.8 %all_gather.3 = bf16[1536,256]{1,0:T(8,128)(2,1)S(1)} all-gather(bf16[96,256]{1,0:T(8,128)(2,1)S(1)} %copy-done), channel_id=1, replica_groups=mesh['row'=16,'col'=32] {'row'}, dimensions={0}, use_global_device_ids=true | all-gather | bytes 835584 | tf_op jit(solution)/shard_map/all_gather | solution.py:34
  87.4 0.0 copy-start.2
  87.4 1.3 convert_element_type.14
  88.7 0.0 copy-done.1
  88.7 0.0 all-to-all-done
  88.7 1.8 bitcast_convert_fusion
  90.5 0.0 copy-done.2
  90.5 0.0 copy-start.3
  90.5 42.3 %while.11 = (s32[]{:T(128)}, f32[8,4]{1,0:T(8,128)S(1)}, f32[8,512,256]{2,1,0:T(8,128)}, f32[1536,256]{1,0:T(8,128)}, f32[1536,512]{1,0:T(8,128)S(1)}, /*index=5...) while((s32[]{:T(128)}, f32[8,4]{1,0:T(8,128)S(1)}, f32[8,512,256]{2,1,0:T(8,128)}, ...), condition=%wide.region_2.3_spmd.clone, body=%wide.region_0.2_spmd.clone.sunk | while | flops 2417576448 | bytes 5280401 | solution.py:43
  90.5 4.4 %fusion.27 = f32[1536]{0:T(1024)S(1)} fusion(f32[1536,512]{1,0:T(8,128)S(1)} %get-tuple-element.135, f32[1536,256]{1,0:T(8,128)} %get-tuple-element.134, f32[8,512,256]{2,1,0:T(8,128)} %get-tuple-element.133, s32[]{:T(128)} %get-tuple-element.122), kind=kOutput, calls=%fused_computation.3.clone.1 | convolution fusion | flops 2417490432 | bytes 5249536 | tf_op jit(solution)/shard_map/while/body/eval_jaxpr/dot_general | solution.py:37
  95.0 0.8 fusion.28
  95.8 4.4 %fusion.27 = f32[1536]{0:T(1024)S(1)} fusion(f32[1536,512]{1,0:T(8,128)S(1)} %get-tuple-element.135, f32[1536,256]{1,0:T(8,128)} %get-tuple-element.134, f32[8,512,256]{2,1,0:T(8,128)} %get-tuple-element.133, s32[]{:T(128)} %get-tuple-element.122), kind=kOutput, calls=%fused_computation.3.clone.1 | convolution fusion | flops 2417490432 | bytes 5249536 | tf_op jit(solution)/shard_map/while/body/eval_jaxpr/dot_general | solution.py:37
  100.2 0.8 fusion.28
  101.1 4.4 %fusion.27 = f32[1536]{0:T(1024)S(1)} fusion(f32[1536,512]{1,0:T(8,128)S(1)} %get-tuple-element.135, f32[1536,256]{1,0:T(8,128)} %get-tuple-element.134, f32[8,512,256]{2,1,0:T(8,128)} %get-tuple-element.133, s32[]{:T(128)} %get-tuple-element.122), kind=kOutput, calls=%fused_computation.3.clone.1 | convolution fusion | flops 2417490432 | bytes 5249536 | tf_op jit(solution)/shard_map/while/body/eval_jaxpr/dot_general | solution.py:37
  105.5 0.8 fusion.28
  106.4 4.4 %fusion.27 = f32[1536]{0:T(1024)S(1)} fusion(f32[1536,512]{1,0:T(8,128)S(1)} %get-tuple-element.135, f32[1536,256]{1,0:T(8,128)} %get-tuple-element.134, f32[8,512,256]{2,1,0:T(8,128)} %get-tuple-element.133, s32[]{:T(128)} %get-tuple-element.122), kind=kOutput, calls=%fused_computation.3.clone.1 | convolution fusion | flops 2417490432 | bytes 5249536 | tf_op jit(solution)/shard_map/while/body/eval_jaxpr/dot_general | solution.py:37
  110.8 0.8 fusion.28
  111.7 4.4 %fusion.27 = f32[1536]{0:T(1024)S(1)} fusion(f32[1536,512]{1,0:T(8,128)S(1)} %get-tuple-element.135, f32[1536,256]{1,0:T(8,128)} %get-tuple-element.134, f32[8,512,256]{2,1,0:T(8,128)} %get-tuple-element.133, s32[]{:T(128)} %get-tuple-element.122), kind=kOutput, calls=%fused_computation.3.clone.1 | convolution fusion | flops 2417490432 | bytes 5249536 | tf_op jit(solution)/shard_map/while/body/eval_jaxpr/dot_general | solution.py:37
  116.1 0.8 fusion.28
  117.0 4.4 %fusion.27 = f32[1536]{0:T(1024)S(1)} fusion(f32[1536,512]{1,0:T(8,128)S(1)} %get-tuple-element.135, f32[1536,256]{1,0:T(8,128)} %get-tuple-element.134, f32[8,512,256]{2,1,0:T(8,128)} %get-tuple-element.133, s32[]{:T(128)} %get-tuple-element.122), kind=kOutput, calls=%fused_computation.3.clone.1 | convolution fusion | flops 2417490432 | bytes 5249536 | tf_op jit(solution)/shard_map/while/body/eval_jaxpr/dot_general | solution.py:37
  121.4 0.8 fusion.28
  122.3 4.4 %fusion.27 = f32[1536]{0:T(1024)S(1)} fusion(f32[1536,512]{1,0:T(8,128)S(1)} %get-tuple-element.135, f32[1536,256]{1,0:T(8,128)} %get-tuple-element.134, f32[8,512,256]{2,1,0:T(8,128)} %get-tuple-element.133, s32[]{:T(128)} %get-tuple-element.122), kind=kOutput, calls=%fused_computation.3.clone.1 | convolution fusion | flops 2417490432 | bytes 5249536 | tf_op jit(solution)/shard_map/while/body/eval_jaxpr/dot_general | solution.py:37
  126.7 0.8 fusion.28
  127.6 4.4 %fusion.27 = f32[1536]{0:T(1024)S(1)} fusion(f32[1536,512]{1,0:T(8,128)S(1)} %get-tuple-element.135, f32[1536,256]{1,0:T(8,128)} %get-tuple-element.134, f32[8,512,256]{2,1,0:T(8,128)} %get-tuple-element.133, s32[]{:T(128)} %get-tuple-element.122), kind=kOutput, calls=%fused_computation.3.clone.1 | convolution fusion | flops 2417490432 | bytes 5249536 | tf_op jit(solution)/shard_map/while/body/eval_jaxpr/dot_general | solution.py:37
  132.0 0.8 fusion.28
  132.8 106.2 %psum.7 = f32[8,4]{1,0:T(8,128)S(1)} all-reduce(f32[8,4]{1,0:T(8,128)S(1)} %get-tuple-element.37), channel_id=1, replica_groups=mesh['row'=16,'col'=32] {'row','col'}, use_global_device_ids=true, to_apply=%region_3.4 | all-reduce | flops 32 | bytes 256 | tf_op jit(solution)/shard_map/psum | solution.py:44
  239.0 0.0 copy-done.3
  239.1 0.8 convolution_multiply_fusion
  (18 shorter events, 0.3 us)
Async XLA Ops:
  0.0 19.6 %copy-start = (bf16[96,256]{1,0:T(8,128)(2,1)S(1)}, bf16[96,256]{1,0:T(8,128)(2,1)}, u32[]{:S(2)}) copy-start(bf16[96,256]{1,0:T(8,128)(2,1)} %param.10) | copy-start | bytes 147460
  2.1 86.5 %copy-start.1 = (s32[1536]{0:T(1024)S(1)}, s32[1536]{0:T(1024)}, u32[]{:S(2)}) copy-start(s32[1536]{0:T(1024)} %param.11) | copy-start | bytes 18436
  2.1 86.5 %all-to-all-start = ((bf16[32,48,512]{2,1,0:T(8,128)(2,1)}), bf16[32,48,512]{2,1,0:T(8,128)(2,1)}, u32[]{:S(2)}, u32[]{:S(2)}) async-start(bf16[32,48,512]{2,1,0:T(8,128)(2,1)} %stack.2), calls=%async_computation | async-start | bytes 3145728 | tf_op jit(solution)/shard_map/all_to_all | solution.py:16
  87.4 3.1 %copy-start.2 = (s32[1536]{0:T(1024)S(1)}, s32[1536]{0:T(1024)}, u32[]{:S(2)}) copy-start(s32[1536]{0:T(1024)} %param.12) | copy-start | bytes 18436
  90.5 148.5 %copy-start.3 = (s32[8]{0:T(128)S(1)}, s32[8]{0:T(128)}, u32[]{:S(2)}) copy-start(s32[8]{0:T(128)} %param.13) | copy-start | bytes 100
